TPU v7x, 256 devices: a whole 4x4x8 slice. The times are simulated.
256 devices in a mesh: row: 8 (over x, core), col: 32 (over y, z).
Axes of the slice: x: 4, y: 4, z: 8, core: 2. Of those that a mesh axis runs over, the one named last changes fastest.
Arguments:
- tokens: bfloat16 [1024, 6144], P('col', 'row'), may hold values from -6 to 6
- w_up: bfloat16 [6144, 24576], P('row', 'col'), may hold values from -0.078125 to 0.078125
- w_down: bfloat16 [24576, 6144], P('col', 'row'), may hold values from -0.0390625 to 0.0390625
- expert_in: bfloat16 [6144, 8192], P(None, 'col'), may hold values from -0.078125 to 0.078125
- expert_out: bfloat16 [8192, 6144], P('col'), may hold values from -0.125 to 0.125
- expert_ids: int32 [1024, 2], P('col'), may hold values from 0 to 3, as said below
- route_weights: bfloat16 [1024, 2], P('col'), may hold values from 0.25 to 1
- out_grad: bfloat16 [1024, 6144], P('col', 'row'), may hold values from -6 to 6
Outputs:
- layer_out: bfloat16 [1024, 6144], P('col', 'row')
- tokens_grad: bfloat16 [1024, 6144], P('col', 'row')
- up_grad: bfloat16 [6144, 24576], P('row', 'col')
- down_grad: bfloat16 [24576, 6144], P('col', 'row')
- expert_in_grad: bfloat16 [6144, 8192], P('row', 'col')
- expert_out_grad: bfloat16 [8192, 6144], P('col', 'row')
Inputs may be any that keep to these rules, and one draw needn't show every extreme that they name: `expert_ids`: the two experts of a token differ. In every aligned block of 4 tokens no expert is named by more than 3 of the block's pairs; one expert is named by exactly 3 pairs, the same expert in all blocks whose index leaves the same remainder modulo 32 // 4; the other experts' counts in a block differ by at most one. Every expert is named somewhere.
All inputs are finite; a program needn't handle non-finite values.
Results may differ from a plain program's by a relative error of at most 0.025.
Values may be sent and summed in bfloat16 or wider, within the bound.
No kernel may reach another device: no remote copies, remote signals or barrier semaphores. Data moves between devices by JAX's collectives and lax.ppermute only.
A program may use at most 128 MiB of HBM per device.

v0:
```python
import jax
import jax.numpy as jnp
from jax import lax
from jax.sharding import PartitionSpec as P

EXPERTS = 4
gelu_scale = 0.7978845608028654
gelu_cubic = 0.044715


def gelu_tanh(value):
    return 0.5 * value * (1.0 + jnp.tanh(gelu_scale * (value + gelu_cubic * value * value * value)))


def gelu_slope(value):
    inner = jnp.tanh(gelu_scale * (value + gelu_cubic * value * value * value))
    return 0.5 * (1.0 + inner) + 0.5 * value * (1.0 - inner * inner) * gelu_scale * (
        1.0 + 3.0 * gelu_cubic * value * value
    )


def slot_ranks(pairs):
    count = pairs.shape[-1]
    positions = jnp.arange(count, dtype=jnp.int32)
    earlier = positions[:, None] > positions[None, :]
    matching = pairs[..., :, None] == pairs[..., None, :]
    return jnp.sum((matching & earlier).astype(jnp.int32), axis=-1)


def on_device(tokens, w_up, w_down, expert_in, expert_out, expert_ids, route_weights, out_grad):
    row_count = lax.axis_size("row")
    col_count = lax.axis_size("col")
    tok_col = tokens.shape[0]
    block_len = tok_col // row_count
    group_len = col_count // EXPERTS
    slot_cap = max(2, 3 * block_len // 4)
    model_width = expert_out.shape[1]
    my_row = lax.axis_index("row")
    tok_panel = lax.all_gather(tokens, "col", axis=0, tiled=True)
    up_terms = jnp.dot(tok_panel, w_up, preferred_element_type=jnp.float32)
    preact = lax.psum_scatter(
        up_terms.astype(jnp.bfloat16), "row", scatter_dimension=0, tiled=True
    ).astype(jnp.float32)
    hidden_full = lax.all_gather(gelu_tanh(preact).astype(jnp.bfloat16), "row", axis=0, tiled=True)
    rows_in = hidden_full
    dense_term = lax.psum_scatter(
        jnp.dot(rows_in, w_down, preferred_element_type=jnp.float32).astype(jnp.bfloat16),
        "col",
        scatter_dimension=0,
        tiled=True,
    ).astype(jnp.float32)
    mixed_act = (tokens.astype(jnp.float32) + dense_term).astype(jnp.bfloat16)
    own_rows, own_grad = (
        lax.all_to_all(mixed_act, "row", split_axis=0, concat_axis=1, tiled=True),
        lax.all_to_all(out_grad, "row", split_axis=0, concat_axis=1, tiled=True),
    )
    chosen = lax.dynamic_slice_in_dim(expert_ids, my_row * block_len, block_len, 0).reshape(-1)
    weights_own = lax.dynamic_slice_in_dim(route_weights, my_row * block_len, block_len, 0)
    weights_flat = weights_own.reshape(-1).astype(jnp.float32)
    rows_x = jnp.repeat(own_rows, 2, axis=0)
    scaled = (weights_flat[:, None] * jnp.repeat(own_grad, 2, axis=0).astype(jnp.float32)).astype(
        jnp.bfloat16
    )
    slot_range = jnp.arange(slot_cap, dtype=jnp.int32)
    placed = slot_ranks(chosen)
    expert_range = jnp.arange(EXPERTS, dtype=jnp.int32)
    onehot = (
        (chosen[None, None, :] == expert_range[:, None, None])
        & (placed[None, None, :] == slot_range[None, :, None])
    ).astype(jnp.bfloat16)
    send_x = jnp.einsum("eca,ad->ecd", onehot, rows_x, preferred_element_type=jnp.float32).astype(
        jnp.bfloat16
    )
    send_g = jnp.einsum("eca,ad->ecd", onehot, scaled, preferred_element_type=jnp.float32).astype(
        jnp.bfloat16
    )
    send_x = jnp.repeat(send_x, group_len, axis=0)
    send_g = jnp.repeat(send_g, group_len, axis=0)
    got_x, got_g = (
        lax.all_to_all(send_x, "col", split_axis=0, concat_axis=0, tiled=True),
        lax.all_to_all(send_g, "col", split_axis=0, concat_axis=0, tiled=True),
    )
    inputs = got_x.reshape(-1, model_width)
    grads = got_g.reshape(-1, model_width)
    e_pre = jnp.dot(inputs, expert_in, preferred_element_type=jnp.float32)
    e_hidden = gelu_tanh(e_pre).astype(jnp.bfloat16)
    values = jnp.dot(e_hidden, expert_out, preferred_element_type=jnp.float32)
    e_dpre = (
        jnp.dot(grads, expert_out.T, preferred_element_type=jnp.float32) * gelu_slope(e_pre)
    ).astype(jnp.bfloat16)
    returns = jnp.dot(e_dpre, expert_in.T, preferred_element_type=jnp.float32)
    grad_in = jnp.dot(inputs.T, e_dpre, preferred_element_type=jnp.float32)
    grad_out = jnp.dot(e_hidden.T, grads, preferred_element_type=jnp.float32)
    values, returns, grad_in, grad_out = (values, returns, grad_in, grad_out)
    back_v, back_d = (
        lax.all_to_all(
            values.reshape(col_count, slot_cap, model_width).astype(jnp.bfloat16),
            "col",
            split_axis=0,
            concat_axis=0,
            tiled=True,
        ).astype(jnp.float32),
        lax.all_to_all(
            returns.reshape(col_count, slot_cap, model_width).astype(jnp.bfloat16),
            "col",
            split_axis=0,
            concat_axis=0,
            tiled=True,
        ).astype(jnp.float32),
    )
    flat_v = (
        back_v.reshape(EXPERTS, group_len, slot_cap, model_width)
        .sum(axis=1)
        .reshape(EXPERTS * slot_cap, model_width)
    )
    flat_d = (
        back_d.reshape(EXPERTS, group_len, slot_cap, model_width)
        .sum(axis=1)
        .reshape(EXPERTS * slot_cap, model_width)
    )
    lookup = chosen * slot_cap + placed
    moe_sum = (
        (weights_flat[:, None] * jnp.take(flat_v, lookup, axis=0))
        .reshape(block_len, 2, model_width)
        .sum(axis=1)
    )
    grad_sum = jnp.take(flat_d, lookup, axis=0).reshape(block_len, 2, model_width).sum(axis=1)
    layer_rows = (own_rows.astype(jnp.float32) + moe_sum).astype(jnp.bfloat16)
    grad_rows = (own_grad.astype(jnp.float32) + grad_sum).astype(jnp.bfloat16)
    layer_out, mixed_grad = (
        lax.all_to_all(layer_rows, "row", split_axis=1, concat_axis=0, tiled=True),
        lax.all_to_all(grad_rows, "row", split_axis=1, concat_axis=0, tiled=True),
    )
    expert_in_grad = lax.psum_scatter(
        grad_in.astype(jnp.bfloat16), "row", scatter_dimension=0, tiled=True
    )
    expert_out_grad = lax.psum_scatter(
        grad_out.astype(jnp.bfloat16), "row", scatter_dimension=1, tiled=True
    )
    cot_panel = lax.all_gather(mixed_grad, "col", axis=0, tiled=True)
    hgrad_terms = jnp.dot(cot_panel, w_down.T, preferred_element_type=jnp.float32)
    down_grad = jnp.dot(hidden_full.T, cot_panel, preferred_element_type=jnp.float32).astype(
        jnp.bfloat16
    )
    hidden_grad = lax.psum_scatter(
        hgrad_terms.astype(jnp.bfloat16), "row", scatter_dimension=0, tiled=True
    ).astype(jnp.float32)
    dpre_full = lax.all_gather(
        (hidden_grad * gelu_slope(preact)).astype(jnp.bfloat16), "row", axis=0, tiled=True
    )
    up_grad = jnp.dot(tok_panel.T, dpre_full, preferred_element_type=jnp.float32).astype(
        jnp.bfloat16
    )
    rows_in = dpre_full
    input_term = lax.psum_scatter(
        jnp.dot(rows_in, w_up.T, preferred_element_type=jnp.float32).astype(jnp.bfloat16),
        "col",
        scatter_dimension=0,
        tiled=True,
    ).astype(jnp.float32)
    tokens_grad = (mixed_grad.astype(jnp.float32) + input_term).astype(jnp.bfloat16)
    return (layer_out, tokens_grad, up_grad, down_grad, expert_in_grad, expert_out_grad)


def solution(mesh):
    in_specs = (
        P("col", "row"),
        P("row", "col"),
        P("col", "row"),
        P(None, "col"),
        P("col", None),
        P("col", None),
        P("col", None),
        P("col", "row"),
    )
    out_specs = (
        P("col", "row"),
        P("col", "row"),
        P("row", "col"),
        P("col", "row"),
        P("row", "col"),
        P("col", "row"),
    )
    return jax.shard_map(
        on_device, mesh=mesh, in_specs=in_specs, out_specs=out_specs, check_vma=False
    )
```

profile of v0, /device:TPU:8, one launch (start us, length us, event | category | flops | bytes accessed | tf_op | source)
XLA Modules:
  0.0 1058.8 jit_solution(8834172341026235586)
XLA Ops:
  8.0 81.4 %all-gather.5.cloned.1.call-done = bf16[1024,768]{1,0:T(8,128)(2,1)} async-done(((bf16[32,768]{1,0:T(8,128)(2,1)}), bf16[1024,768]{1,0:T(8,128)(2,1)}) %all-gather.5.cloned.1.call-update) | async-done | bytes 1572880 | tf_op jit(solution)/shard_map/all_gather | solution.py:39
  89.4 4.3 convolution_convert_fusion.9
  93.8 34.1 %reduce-scatter.7.cloned.1.call-done = bf16[128,768]{1,0:T(8,128)(2,1)} async-done(((bf16[1024,768]{1,0:T(8,128)(2,1)}), bf16[128,768]{1,0:T(8,128)(2,1)}) %reduce-scatter.7.cloned.1.call-update) | async-done | bytes 196624 | tf_op jit(solution)/shard_map/reduce_scatter | solution.py:41
  129.6 26.3 %all-gather.7.cloned.1.call-done = bf16[1024,768]{1,0:T(8,128)(2,1)} async-done(((bf16[128,768]{1,0:T(8,128)(2,1)}), bf16[1024,768]{1,0:T(8,128)(2,1)}) %all-gather.7.cloned.1.call-update) | async-done | bytes 1572880 | tf_op jit(solution)/shard_map/all_gather | solution.py:44
  156.0 4.3 convolution_convert_fusion.8
  166.3 4.2 all-to-all-done.4
  171.4 207.3 %reduce-scatter.9.cloned.1.call-done = bf16[32,768]{1,0:T(8,128)(2,1)} async-done(((bf16[1024,768]{1,0:T(8,128)(2,1)}), bf16[32,768]{1,0:T(8,128)(2,1)}) %reduce-scatter.9.cloned.1.call-update) | async-done | bytes 49168 | tf_op jit(solution)/shard_map/reduce_scatter | solution.py:46
  380.1 4.2 all-to-all-start
  384.8 5.2 all-to-all-done
  391.9 8.0 all-to-all-start.5
  401.1 35.5 %all-to-all-done.5 = bf16[32,3,6144]{2,1,0:T(4,128)(2,1)} async-done(((bf16[32,3,6144]{2,1,0:T(4,128)(2,1)}), bf16[32,3,6144]{2,1,0:T(4,128)(2,1)}, u32[]{:S(2)}, u32[]{:S(2)}) %all-to-all-start.5) | async-done | bytes 1179680 | tf_op jit(solution)/shard_map/all_to_all | solution.py:81
  438.5 8.2 all-to-all-start.1
  446.7 4.0 reshape.146
  450.7 32.5 %all-to-all-done.1 = bf16[32,3,6144]{2,1,0:T(4,128)(2,1)} async-done(((bf16[32,3,6144]{2,1,0:T(4,128)(2,1)}), bf16[32,3,6144]{2,1,0:T(4,128)(2,1)}, u32[]{:S(2)}, u32[]{:S(2)}) %all-to-all-start.1) | async-done | bytes 1179680 | tf_op jit(solution)/shard_map/all_to_all | solution.py:80
  483.2 3.9 reshape.140
  497.3 8.1 all-to-all-start.6
  512.9 29.0 %all-to-all-done.6 = bf16[32,3,6144]{2,1,0:T(4,128)(2,1)} async-done(((bf16[32,3,6144]{2,1,0:T(4,128)(2,1)}), bf16[32,3,6144]{2,1,0:T(4,128)(2,1)}, u32[]{:S(2)}, u32[]{:S(2)}) %all-to-all-start.6) | async-done | bytes 1179680 | tf_op jit(solution)/shard_map/all_to_all | solution.py:103
  541.9 8.1 all-to-all-start.2
  554.4 32.1 %all-to-all-done.2 = bf16[32,3,6144]{2,1,0:T(4,128)(2,1)} async-done(((bf16[32,3,6144]{2,1,0:T(4,128)(2,1)}), bf16[32,3,6144]{2,1,0:T(4,128)(2,1)}, u32[]{:S(2)}, u32[]{:S(2)}) %all-to-all-start.2) | async-done | bytes 1179680 | tf_op jit(solution)/shard_map/all_to_all | solution.py:96
  599.5 7.9 all_to_all.84
  608.1 73.4 %all-gather.9.cloned.1.call-done = bf16[1024,768]{1,0:T(8,128)(2,1)} async-done(((bf16[32,768]{1,0:T(8,128)(2,1)}), bf16[1024,768]{1,0:T(8,128)(2,1)}) %all-gather.9.cloned.1.call-update) | async-done | bytes 1572880 | tf_op jit(solution)/shard_map/all_gather | solution.py:140
  681.5 4.3 convolution_convert_fusion.7
  685.9 34.2 %reduce-scatter.11.cloned.1.call-done = bf16[128,768]{1,0:T(8,128)(2,1)} async-done(((bf16[1024,768]{1,0:T(8,128)(2,1)}), bf16[128,768]{1,0:T(8,128)(2,1)}) %reduce-scatter.11.cloned.1.call-update) | async-done | bytes 196624 | tf_op jit(solution)/shard_map/reduce_scatter | solution.py:145
  722.1 26.1 %all-gather.11.cloned.1.call-done = bf16[1024,768]{1,0:T(8,128)(2,1)} async-done(((bf16[128,768]{1,0:T(8,128)(2,1)}), bf16[1024,768]{1,0:T(8,128)(2,1)}) %all-gather.11.cloned.1.call-update) | async-done | bytes 1572880 | tf_op jit(solution)/shard_map/all_gather | solution.py:148
  748.1 4.3 convolution_convert_fusion.6
  753.4 3.9 convolution_convert_fusion
  758.1 4.0 convolution_convert_fusion.1
  763.3 8.6 all_to_all.85
  772.5 4.5 convolution_convert_fusion.10
  781.8 188.9 %reduce-scatter.13.cloned.1.call-done = bf16[32,768]{1,0:T(8,128)(2,1)} async-done(((bf16[1024,768]{1,0:T(8,128)(2,1)}), bf16[32,768]{1,0:T(8,128)(2,1)}) %reduce-scatter.13.cloned.1.call-update) | async-done | bytes 49168 | tf_op jit(solution)/shard_map/reduce_scatter | solution.py:155
  972.2 39.5 %reduce-scatter.17.cloned.1.call-done = bf16[256,768]{1,0:T(8,128)(2,1)} async-done(((bf16[256,6144]{1,0:T(8,128)(2,1)}), bf16[256,768]{1,0:T(8,128)(2,1)}) %reduce-scatter.17.cloned.1.call-update) | async-done | bytes 393232 | tf_op jit(solution)/shard_map/reduce_scatter | solution.py:137
  1011.6 40.3 %reduce-scatter.15.cloned.1.call-done = bf16[768,256]{1,0:T(8,128)(2,1)} async-done(((bf16[6144,256]{1,0:T(8,128)(2,1)}), bf16[768,256]{1,0:T(8,128)(2,1)}) %reduce-scatter.15.cloned.1.call-update) | async-done | bytes 393232 | tf_op jit(solution)/shard_map/reduce_scatter | solution.py:134
  (108 shorter events, 63.7 us)
Async XLA Ops:
  7.2 479.9 %copy-start = (bf16[6144,256]{1,0:T(8,128)(2,1)S(1)}, bf16[6144,256]{1,0:T(8,128)(2,1)}, u32[]{:S(2)}) copy-start(bf16[6144,256]{1,0:T(8,128)(2,1)} %param.13) | copy-start | bytes 9437188
  7.2 82.2 %all-gather.5.cloned.1.call-start = ((), (), s32[]{:S(2)}) async-start(), calls=%async_computation.14 | async-start | bytes 1622016 | tf_op jit(solution)/shard_map/all_gather | solution.py:39
  7.9 119.9 %reduce-scatter.7.cloned.1.call-start = ((), (), s32[]{:S(2)}) async-start(), calls=%async_computation.15 | async-start | bytes 1769472 | tf_op jit(solution)/shard_map/reduce_scatter | solution.py:41
  93.7 62.3 %all-gather.7.cloned.1.call-start = ((), (), s32[]{:S(2)}) async-start(), calls=%async_computation.16 | async-start | bytes 1769472 | tf_op jit(solution)/shard_map/all_gather | solution.py:44
  129.6 249.0 %reduce-scatter.9.cloned.1.call-start = ((), (), s32[]{:S(2)}) async-start(), calls=%async_computation.17 | async-start | bytes 1622016 | tf_op jit(solution)/shard_map/reduce_scatter | solution.py:46
  160.3 0.8 copy-start.11
  160.3 4.8 copy-start.12
  160.3 5.8 copy-start.13
  161.7 8.8 all-to-all-start.4
  170.5 0.6 copy-start.10
  380.1 9.9 all-to-all-start
  391.9 44.8 %all-to-all-start.5 = ((bf16[32,3,6144]{2,1,0:T(4,128)(2,1)}), bf16[32,3,6144]{2,1,0:T(4,128)(2,1)}, u32[]{:S(2)}, u32[]{:S(2)}) async-start(bf16[32,3,6144]{2,1,0:T(4,128)(2,1)} %bitcast.50), calls=%async_computation.7 | async-start | bytes 3145728 | tf_op jit(solution)/shard_map/all_to_all | solution.py:81
  438.5 44.6 %all-to-all-start.1 = ((bf16[32,3,6144]{2,1,0:T(4,128)(2,1)}), bf16[32,3,6144]{2,1,0:T(4,128)(2,1)}, u32[]{:S(2)}, u32[]{:S(2)}) async-start(bf16[32,3,6144]{2,1,0:T(4,128)(2,1)} %bitcast.51), calls=%async_computation.3 | async-start | bytes 3145728 | tf_op jit(solution)/shard_map/all_to_all | solution.py:80
  487.1 2.2 copy-start.1
  487.1 2.6 copy-start.2
  489.7 15.8 %copy-start.3 = (f32[96,256]{1,0:T(8,128)}, f32[96,256]{1,0:T(8,128)S(1)}, u32[]{:S(2)}) copy-start(f32[96,256]{1,0:T(8,128)S(1)} %fusion.29) | copy-start | bytes 294916
  497.3 44.6 %all-to-all-start.6 = ((bf16[32,3,6144]{2,1,0:T(4,128)(2,1)}), bf16[32,3,6144]{2,1,0:T(4,128)(2,1)}, u32[]{:S(2)}, u32[]{:S(2)}) async-start(bf16[32,3,6144]{2,1,0:T(4,128)(2,1)} %convert_element_type.155), calls=%async_computation.8 | async-start | bytes 3145728 | tf_op jit(solution)/shard_map/all_to_all | solution.py:103
  512.8 37.4 %copy-start.15 = (s32[8]{0:T(128)S(1)}, s32[8]{0:T(128)}, u32[]{:S(2)}) copy-start(s32[8]{0:T(128)} %copy-done.14) | copy-start | bytes 100
  541.9 44.6 %all-to-all-start.2 = ((bf16[32,3,6144]{2,1,0:T(4,128)(2,1)}), bf16[32,3,6144]{2,1,0:T(4,128)(2,1)}, u32[]{:S(2)}, u32[]{:S(2)}) async-start(bf16[32,3,6144]{2,1,0:T(4,128)(2,1)} %convert_element_type.144), calls=%async_computation.4 | async-start | bytes 3145728 | tf_op jit(solution)/shard_map/all_to_all | solution.py:96
  550.0 131.5 %all-gather.9.cloned.1.call-start = ((), (), s32[]{:S(2)}) async-start(), calls=%async_computation.18 | async-start | bytes 1622016 | tf_op jit(solution)/shard_map/all_gather | solution.py:140
  592.5 2.4 copy-start.6
  608.1 112.0 %reduce-scatter.11.cloned.1.call-start = ((), (), s32[]{:S(2)}) async-start(), calls=%async_computation.19 | async-start | bytes 1769472 | tf_op jit(solution)/shard_map/reduce_scatter | solution.py:145
  685.9 34.2 %copy-start.5 = (bf16[128,768]{1,0:T(8,128)(2,1)S(1)}, bf16[128,768]{1,0:T(8,128)(2,1)}, u32[]{:S(2)}) copy-start(bf16[128,768]{1,0:T(8,128)(2,1)} %reduce-scatter.7.cloned.1.call-done) | copy-start | bytes 589828
  685.9 62.2 %all-gather.11.cloned.1.call-start = ((), (), s32[]{:S(2)}) async-start(), calls=%async_computation.20 | async-start | bytes 1769472 | tf_op jit(solution)/shard_map/all_gather | solution.py:148
  722.0 248.7 %reduce-scatter.13.cloned.1.call-start = ((), (), s32[]{:S(2)}) async-start(), calls=%async_computation.21 | async-start | bytes 1622016 | tf_op jit(solution)/shard_map/reduce_scatter | solution.py:155
  752.5 0.9 copy-start.4
  752.5 259.1 %reduce-scatter.17.cloned.1.call-start = ((), (), s32[]{:S(2)}) async-start(), calls=%async_computation.23 | async-start | bytes 3538944 | tf_op jit(solution)/shard_map/reduce_scatter | solution.py:137
  757.3 0.8 copy-start.8
  757.3 294.6 %reduce-scatter.15.cloned.1.call-start = ((), (), s32[]{:S(2)}) async-start(), calls=%async_computation.22 | async-start | bytes 3538944 | tf_op jit(solution)/shard_map/reduce_scatter | solution.py:134
  772.5 4.5 copy-start.16
  772.5 4.5 copy-start.17
  779.4 191.3 %copy-start.9 = (bf16[32,768]{1,0:T(8,128)(2,1)S(1)}, bf16[32,768]{1,0:T(8,128)(2,1)}, u32[]{:S(2)}) copy-start(bf16[32,768]{1,0:T(8,128)(2,1)} %all_to_all.75) | copy-start | bytes 147460
  (2 other events, 1.1 us)
Sparse Core Ops, SparseCore 0:
  10.6 78.7 all-gather.4
  93.8 33.9 reduce-scatter.6
  130.2 25.6 all-gather.6
  160.4 218.1 reduce-scatter.8
  608.2 73.2 all-gather.8
  686.0 34.0 reduce-scatter.10
  722.5 25.5 all-gather.10
  752.6 218.0 reduce-scatter.12
  973.9 37.7 reduce-scatter.16
  1014.6 37.3 reduce-scatter.14
where the time goes:
time: 1060 us
  waiting for transfers between devices  891 us (84%)
  matrix products  41.5 us (4%)
  starting transfers between devices  40.6 us (4%)
  local copies, waits for them, and re-layouts  38.4 us (4%)
  other arithmetic  16.7 us (2%)
  blocking collectives  16.5 us (2%)
  between operations  14.4 us (1%)
    reduce_scatter x1, waiting for transfers between devices, on_device(): lax.psum_scatter(jnp.dot(rows_in, w_down, preferred_element_type=jnp.floa...  207 us
    reduce_scatter x1, waiting for transfers between devices, on_device(): lax.psum_scatter(jnp.dot(rows_in, w_up.T, preferred_element_type=jnp.floa...  189 us
    all_gather x1, waiting for transfers between devices, on_device(): tok_panel = lax.all_gather(tokens, 'col', axis=0, tiled=True)  81.4 us
    all_gather x1, waiting for transfers between devices, on_device(): cot_panel = lax.all_gather(mixed_grad, 'col', axis=0, tiled=True)  73.4 us
    reduce_scatter x1, waiting for transfers between devices, on_device(): lax.psum_scatter(grad_in.astype(jnp.bfloat16), 'row', scatter_dimension=0...  40.3 us
    reduce_scatter x1, waiting for transfers between devices, on_device(): lax.psum_scatter(grad_out.astype(jnp.bfloat16), 'row', scatter_dimension=...  39.5 us
    all_to_all x1, waiting for transfers between devices, on_device(): lax.all_to_all(send_g, 'col', split_axis=0, concat_axis=0, tiled=True)  35.5 us
    reduce_scatter x1, waiting for transfers between devices, on_device(): lax.psum_scatter(hgrad_terms.astype(jnp.bfloat16), 'row', scatter_dimensi...  34.2 us
  transfers between devices with their start and end apart: 16, of which 16 were waited for; matrix products, arithmetic and copies ran while one was open for 4% of the time, Pallas kernels for 0%

commit v1 on v0

--- a/solution.py
+++ b/solution.py
@@ -145,9 +145,16 @@
     hidden_grad = lax.psum_scatter(
         hgrad_terms.astype(jnp.bfloat16), "row", scatter_dimension=0, tiled=True
     ).astype(jnp.float32)
-    dpre_full = lax.all_gather(
-        (hidden_grad * gelu_slope(preact)).astype(jnp.bfloat16), "row", axis=0, tiled=True
+    frame_expand = lambda slab_in, comm_axis, dim_no: jnp.concatenate(
+        lax.all_to_all(
+            jnp.stack([slab_in] * lax.axis_size(comm_axis)),
+            axis_name=comm_axis,
+            split_axis=0,
+            concat_axis=0,
+        ),
+        axis=dim_no,
     )
+    dpre_full = frame_expand((hidden_grad * gelu_slope(preact)).astype(jnp.bfloat16), "row", 0)
     up_grad = jnp.dot(tok_panel.T, dpre_full, preferred_element_type=jnp.float32).astype(
         jnp.bfloat16
     )

time: 1060 us -> 1060 us (level)
  waiting for transfers between devices: 891 us -> 865 us
  blocking collectives: 16.5 us -> 40 us
    all_gather x1 -> x0, waiting for transfers between devices: 26.1 us -> none  [on_device(): lax.all_gather((hidden_grad * gelu_slope(preact)).astype(jnp.bfloat16), '...]
    all_to_all x0 -> x1, blocking collectives: none -> 24.2 us  [on_device(): lax.all_to_all(jnp.stack([slab_in] * lax.axis_size(comm_axis)), axis_name...]
  transfers between devices with their start and end apart: 16 -> 15, of which waited for: 16 -> 15; matrix products, arithmetic and copies ran while one was open for 4% -> 4% of each run, Pallas kernels for 0% -> 0%
where the time goes in v1:
time: 1060 us; the launch traced here: 1050 us
  waiting for transfers between devices  865 us (82%)
  starting transfers between devices  40.6 us (4%)
  blocking collectives  40 us (4%)
  local copies, waits for them, and re-layouts  39.7 us (4%)
  matrix products  39.7 us (4%)
  other arithmetic  16 us (2%)
  between operations  14.1 us (1%)
    reduce_scatter x1, waiting for transfers between devices, on_device(): lax.psum_scatter(jnp.dot(rows_in, w_down, preferred_element_type=jnp.floa...  207 us
    reduce_scatter x1, waiting for transfers between devices, on_device(): lax.psum_scatter(jnp.dot(rows_in, w_up.T, preferred_element_type=jnp.floa...  189 us
    all_gather x1, waiting for transfers between devices, on_device(): tok_panel = lax.all_gather(tokens, 'col', axis=0, tiled=True)  81.4 us
    all_gather x1, waiting for transfers between devices, on_device(): cot_panel = lax.all_gather(mixed_grad, 'col', axis=0, tiled=True)  73.4 us
    reduce_scatter x1, waiting for transfers between devices, on_device(): lax.psum_scatter(grad_in.astype(jnp.bfloat16), 'row', scatter_dimension=0...  40.5 us
    reduce_scatter x1, waiting for transfers between devices, on_device(): lax.psum_scatter(grad_out.astype(jnp.bfloat16), 'row', scatter_dimension=...  39.3 us
    all_to_all x1, waiting for transfers between devices, on_device(): lax.all_to_all(send_g, 'col', split_axis=0, concat_axis=0, tiled=True)  35.5 us
    reduce_scatter x1, waiting for transfers between devices, on_device(): lax.psum_scatter(hgrad_terms.astype(jnp.bfloat16), 'row', scatter_dimensi...  34.1 us
  transfers between devices with their start and end apart: 15, of which 15 were waited for; matrix products, arithmetic and copies ran while one was open for 4% of the time, Pallas kernels for 0%

profile of v1, /device:TPU:8, one launch (start us, length us, event | category | flops | bytes accessed | tf_op | source)
XLA Modules:
  0.0 1054.7 jit_solution(16203622864471059967)
XLA Ops:
  8.0 81.4 %all-gather.4.cloned.1.call-done = bf16[1024,768]{1,0:T(8,128)(2,1)} async-done(((bf16[32,768]{1,0:T(8,128)(2,1)}), bf16[1024,768]{1,0:T(8,128)(2,1)}) %all-gather.4.cloned.1.call-update) | async-done | bytes 1572880 | tf_op jit(solution)/shard_map/all_gather | solution.py:39
  89.4 4.3 convolution_convert_fusion.9
  93.8 34.1 %reduce-scatter.7.cloned.1.call-done = bf16[128,768]{1,0:T(8,128)(2,1)} async-done(((bf16[1024,768]{1,0:T(8,128)(2,1)}), bf16[128,768]{1,0:T(8,128)(2,1)}) %reduce-scatter.7.cloned.1.call-update) | async-done | bytes 196624 | tf_op jit(solution)/shard_map/reduce_scatter | solution.py:41
  129.6 26.3 %all-gather.6.cloned.1.call-done = bf16[1024,768]{1,0:T(8,128)(2,1)} async-done(((bf16[128,768]{1,0:T(8,128)(2,1)}), bf16[1024,768]{1,0:T(8,128)(2,1)}) %all-gather.6.cloned.1.call-update) | async-done | bytes 1572880 | tf_op jit(solution)/shard_map/all_gather | solution.py:44
  156.0 4.3 convolution_convert_fusion.8
  166.3 4.2 all-to-all-done.4
  171.3 207.4 %reduce-scatter.9.cloned.1.call-done = bf16[32,768]{1,0:T(8,128)(2,1)} async-done(((bf16[1024,768]{1,0:T(8,128)(2,1)}), bf16[32,768]{1,0:T(8,128)(2,1)}) %reduce-scatter.9.cloned.1.call-update) | async-done | bytes 49168 | tf_op jit(solution)/shard_map/reduce_scatter | solution.py:46
  380.2 4.2 all-to-all-start
  384.8 5.2 all-to-all-done
  391.9 8.0 all-to-all-start.5
  401.2 35.5 %all-to-all-done.5 = bf16[32,3,6144]{2,1,0:T(4,128)(2,1)} async-done(((bf16[32,3,6144]{2,1,0:T(4,128)(2,1)}), bf16[32,3,6144]{2,1,0:T(4,128)(2,1)}, u32[]{:S(2)}, u32[]{:S(2)}) %all-to-all-start.5) | async-done | bytes 1179680 | tf_op jit(solution)/shard_map/all_to_all | solution.py:81
  438.6 8.2 all-to-all-start.1
  446.8 4.0 reshape.151
  450.8 32.5 %all-to-all-done.1 = bf16[32,3,6144]{2,1,0:T(4,128)(2,1)} async-done(((bf16[32,3,6144]{2,1,0:T(4,128)(2,1)}), bf16[32,3,6144]{2,1,0:T(4,128)(2,1)}, u32[]{:S(2)}, u32[]{:S(2)}) %all-to-all-start.1) | async-done | bytes 1179680 | tf_op jit(solution)/shard_map/all_to_all | solution.py:80
  483.2 3.9 reshape.145
  493.6 3.8 convert_element_type.155
  497.4 8.1 all-to-all-start.6
  513.0 29.0 %all-to-all-done.6 = bf16[32,3,6144]{2,1,0:T(4,128)(2,1)} async-done(((bf16[32,3,6144]{2,1,0:T(4,128)(2,1)}), bf16[32,3,6144]{2,1,0:T(4,128)(2,1)}, u32[]{:S(2)}, u32[]{:S(2)}) %all-to-all-start.6) | async-done | bytes 1179680 | tf_op jit(solution)/shard_map/all_to_all | solution.py:103
  542.0 8.1 all-to-all-start.2
  554.5 32.1 %all-to-all-done.2 = bf16[32,3,6144]{2,1,0:T(4,128)(2,1)} async-done(((bf16[32,3,6144]{2,1,0:T(4,128)(2,1)}), bf16[32,3,6144]{2,1,0:T(4,128)(2,1)}, u32[]{:S(2)}, u32[]{:S(2)}) %all-to-all-start.2) | async-done | bytes 1179680 | tf_op jit(solution)/shard_map/all_to_all | solution.py:96
  599.6 7.9 all_to_all.89
  608.3 73.4 %all-gather.8.cloned.1.call-done = bf16[1024,768]{1,0:T(8,128)(2,1)} async-done(((bf16[32,768]{1,0:T(8,128)(2,1)}), bf16[1024,768]{1,0:T(8,128)(2,1)}) %all-gather.8.cloned.1.call-update) | async-done | bytes 1572880 | tf_op jit(solution)/shard_map/all_gather | solution.py:140
  681.6 4.3 convolution_convert_fusion.7
  686.0 34.1 %reduce-scatter.11.cloned.1.call-done = bf16[128,768]{1,0:T(8,128)(2,1)} async-done(((bf16[1024,768]{1,0:T(8,128)(2,1)}), bf16[128,768]{1,0:T(8,128)(2,1)}) %reduce-scatter.11.cloned.1.call-update) | async-done | bytes 196624 | tf_op jit(solution)/shard_map/reduce_scatter | solution.py:145
  721.5 24.2 %all_to_all.90 = bf16[8,128,768]{2,1,0:T(8,128)(2,1)S(1)} all-to-all(bf16[8,128,768]{2,1,0:T(8,128)(2,1)S(1)} %stack.2), channel_id=1, replica_groups=mesh['row'=8,'col'=32] {'row'}, dimensions={0} | all-to-all | bytes 3145728 | tf_op jit(solution)/shard_map/all_to_all | solution.py:149
  750.3 3.9 convolution_convert_fusion
  755.0 4.0 convolution_convert_fusion.1
  760.2 7.9 all_to_all.91
  768.7 4.5 convolution_convert_fusion.10
  778.1 188.8 %reduce-scatter.13.cloned.1.call-done = bf16[32,768]{1,0:T(8,128)(2,1)} async-done(((bf16[1024,768]{1,0:T(8,128)(2,1)}), bf16[32,768]{1,0:T(8,128)(2,1)}) %reduce-scatter.13.cloned.1.call-update) | async-done | bytes 49168 | tf_op jit(solution)/shard_map/reduce_scatter | solution.py:162
  968.3 39.3 %reduce-scatter.17.cloned.1.call-done = bf16[256,768]{1,0:T(8,128)(2,1)} async-done(((bf16[256,6144]{1,0:T(8,128)(2,1)}), bf16[256,768]{1,0:T(8,128)(2,1)}) %reduce-scatter.17.cloned.1.call-update) | async-done | bytes 393232 | tf_op jit(solution)/shard_map/reduce_scatter | solution.py:137
  1007.6 40.5 %reduce-scatter.15.cloned.1.call-done = bf16[768,256]{1,0:T(8,128)(2,1)} async-done(((bf16[6144,256]{1,0:T(8,128)(2,1)}), bf16[768,256]{1,0:T(8,128)(2,1)}) %reduce-scatter.15.cloned.1.call-update) | async-done | bytes 393232 | tf_op jit(solution)/shard_map/reduce_scatter | solution.py:134
  (111 shorter events, 63.1 us)
Async XLA Ops:
  7.2 480.0 %copy-start = (bf16[6144,256]{1,0:T(8,128)(2,1)S(1)}, bf16[6144,256]{1,0:T(8,128)(2,1)}, u32[]{:S(2)}) copy-start(bf16[6144,256]{1,0:T(8,128)(2,1)} %param.13) | copy-start | bytes 9437188
  7.2 82.2 %all-gather.4.cloned.1.call-start = ((), (), s32[]{:S(2)}) async-start(), calls=%async_computation.15 | async-start | bytes 1622016 | tf_op jit(solution)/shard_map/all_gather | solution.py:39
  7.9 119.9 %reduce-scatter.7.cloned.1.call-start = ((), (), s32[]{:S(2)}) async-start(), calls=%async_computation.16 | async-start | bytes 1769472 | tf_op jit(solution)/shard_map/reduce_scatter | solution.py:41
  93.7 62.3 %all-gather.6.cloned.1.call-start = ((), (), s32[]{:S(2)}) async-start(), calls=%async_computation.17 | async-start | bytes 1769472 | tf_op jit(solution)/shard_map/all_gather | solution.py:44
  129.6 249.1 %reduce-scatter.9.cloned.1.call-start = ((), (), s32[]{:S(2)}) async-start(), calls=%async_computation.18 | async-start | bytes 1622016 | tf_op jit(solution)/shard_map/reduce_scatter | solution.py:46
  160.3 0.8 copy-start.13
  160.3 4.8 copy-start.14
  160.3 5.8 copy-start.15
  161.7 8.8 all-to-all-start.4
  380.2 9.9 all-to-all-start
  391.9 44.8 %all-to-all-start.5 = ((bf16[32,3,6144]{2,1,0:T(4,128)(2,1)}), bf16[32,3,6144]{2,1,0:T(4,128)(2,1)}, u32[]{:S(2)}, u32[]{:S(2)}) async-start(bf16[32,3,6144]{2,1,0:T(4,128)(2,1)} %bitcast.51), calls=%async_computation.7 | async-start | bytes 3145728 | tf_op jit(solution)/shard_map/all_to_all | solution.py:81
  438.6 44.6 %all-to-all-start.1 = ((bf16[32,3,6144]{2,1,0:T(4,128)(2,1)}), bf16[32,3,6144]{2,1,0:T(4,128)(2,1)}, u32[]{:S(2)}, u32[]{:S(2)}) async-start(bf16[32,3,6144]{2,1,0:T(4,128)(2,1)} %bitcast.52), calls=%async_computation.3 | async-start | bytes 3145728 | tf_op jit(solution)/shard_map/all_to_all | solution.py:80
  487.2 2.2 copy-start.1
  487.2 2.6 copy-start.2
  489.8 15.8 %copy-start.5 = (f32[96,256]{1,0:T(8,128)}, f32[96,256]{1,0:T(8,128)S(1)}, u32[]{:S(2)}) copy-start(f32[96,256]{1,0:T(8,128)S(1)} %fusion.29) | copy-start | bytes 294916
  497.4 44.6 %all-to-all-start.6 = ((bf16[32,3,6144]{2,1,0:T(4,128)(2,1)}), bf16[32,3,6144]{2,1,0:T(4,128)(2,1)}, u32[]{:S(2)}, u32[]{:S(2)}) async-start(bf16[32,3,6144]{2,1,0:T(4,128)(2,1)} %convert_element_type.155), calls=%async_computation.8 | async-start | bytes 3145728 | tf_op jit(solution)/shard_map/all_to_all | solution.py:103
  513.0 37.4 %copy-start.17 = (s32[8]{0:T(128)S(1)}, s32[8]{0:T(128)}, u32[]{:S(2)}) copy-start(s32[8]{0:T(128)} %copy-done.16) | copy-start | bytes 100
  542.0 44.6 %all-to-all-start.2 = ((bf16[32,3,6144]{2,1,0:T(4,128)(2,1)}), bf16[32,3,6144]{2,1,0:T(4,128)(2,1)}, u32[]{:S(2)}, u32[]{:S(2)}) async-start(bf16[32,3,6144]{2,1,0:T(4,128)(2,1)} %convert_element_type.144), calls=%async_computation.4 | async-start | bytes 3145728 | tf_op jit(solution)/shard_map/all_to_all | solution.py:96
  550.1 131.5 %all-gather.8.cloned.1.call-start = ((), (), s32[]{:S(2)}) async-start(), calls=%async_computation.19 | async-start | bytes 1622016 | tf_op jit(solution)/shard_map/all_gather | solution.py:140
  592.7 2.4 copy-start.8
  608.2 111.9 %reduce-scatter.11.cloned.1.call-start = ((), (), s32[]{:S(2)}) async-start(), calls=%async_computation.20 | async-start | bytes 1769472 | tf_op jit(solution)/shard_map/reduce_scatter | solution.py:145
  686.0 34.1 %copy-start.7 = (bf16[128,768]{1,0:T(8,128)(2,1)S(1)}, bf16[128,768]{1,0:T(8,128)(2,1)}, u32[]{:S(2)}) copy-start(bf16[128,768]{1,0:T(8,128)(2,1)} %reduce-scatter.7.cloned.1.call-done) | copy-start | bytes 589828
  686.0 280.9 %reduce-scatter.13.cloned.1.call-start = ((), (), s32[]{:S(2)}) async-start(), calls=%async_computation.21 | async-start | bytes 1622016 | tf_op jit(solution)/shard_map/reduce_scatter | solution.py:162
  721.4 25.3 %copy-start.19 = (bf16[768,768]{1,0:T(8,128)(2,1)S(1)}, bf16[768,768]{1,0:T(8,128)(2,1)}, u32[]{:S(2)}) copy-start(bf16[768,768]{1,0:T(8,128)(2,1)} %param.11) | copy-start | bytes 3538948
  745.6 1.2 copy-start.3
  749.4 0.9 copy-start.6
  749.4 258.2 %reduce-scatter.17.cloned.1.call-start = ((), (), s32[]{:S(2)}) async-start(), calls=%async_computation.23 | async-start | bytes 3538944 | tf_op jit(solution)/shard_map/reduce_scatter | solution.py:137
  754.2 0.8 copy-start.10
  754.2 293.9 %reduce-scatter.15.cloned.1.call-start = ((), (), s32[]{:S(2)}) async-start(), calls=%async_computation.22 | async-start | bytes 3538944 | tf_op jit(solution)/shard_map/reduce_scatter | solution.py:134
  768.7 4.5 copy-start.4
  768.7 4.5 copy-start.18
  775.7 191.2 %copy-start.11 = (bf16[32,768]{1,0:T(8,128)(2,1)S(1)}, bf16[32,768]{1,0:T(8,128)(2,1)}, u32[]{:S(2)}) copy-start(bf16[32,768]{1,0:T(8,128)(2,1)} %all_to_all.78) | copy-start | bytes 147460
  (3 other events, 1.8 us)
Sparse Core Ops, SparseCore 0:
  10.6 78.7 all-gather.3
  93.8 33.9 reduce-scatter.6
  130.2 25.6 all-gather.5
  160.4 218.2 reduce-scatter.8
  608.3 73.2 all-gather.7
  686.1 33.9 reduce-scatter.10
  749.5 217.2 reduce-scatter.12
  970.0 37.5 reduce-scatter.16
  1010.8 37.3 reduce-scatter.14
